TPU v7x, 32 devices: a whole 2x2x4 slice. The times are simulated.
32 devices in a mesh: sample: 16 (over z, x, core), block: 2 (over y).
Axes of the slice: x: 2, y: 2, z: 4, core: 2. Of those that a mesh axis runs over, the one named last changes fastest.
Arguments:
- genotype: int32 [16384, 2000], P('sample', 'block'), may hold values from 0 to 2
- allele_freq: float32 [2000], P('block'), may hold values from 0.05 to 0.5
- phenotype: bfloat16 [16384, 16], P('sample'), may hold values from -6 to 6
- shrinkage: float32 [2], replicated, may hold values from 0.05 to 2
- owner_order: int32 [16], replicated, may hold values from 0 to 15, each once
Outputs:
- predictions: bfloat16 [16, 8, 16384], P('block', None, 'sample')
Inputs may be any that keep to these rules, and one draw needn't show every extreme that they name: `owner_order`: each phenotype appears once.
All inputs are finite; a program needn't handle non-finite values.
Results may differ from a plain program's by a relative error of at most 0.0056.
Values may be sent and summed in bfloat16 or wider, within the bound.
No kernel may reach another device: no remote copies, remote signals or barrier semaphores. Data moves between devices by JAX's collectives and lax.ppermute only.
A program may use at most 128 MiB of HBM per device.

v0:
```python
import jax
import jax.numpy as jnp
from jax import lax
from jax.sharding import PartitionSpec as P

SNPS = 500
FOLDS = 5


def standardize(genotype, allele_freq):
    spread = jnp.sqrt(2.0 * allele_freq * (1.0 - allele_freq))
    return ((genotype.astype(jnp.float32) - 2.0 * allele_freq) / spread).astype(jnp.bfloat16)


def solve_pair(factor, target):
    return jax.scipy.linalg.cho_solve((factor, True), target)


def predict(columns, weights):
    stacked = jnp.transpose(weights, (2, 0, 1)).reshape(-1, weights.shape[1])
    product = lax.dot_general(
        stacked, columns, (((1,), (1,)), ((), ())), preferred_element_type=jnp.float32
    )
    return product.astype(jnp.bfloat16).reshape(
        weights.shape[2], weights.shape[0], columns.shape[0]
    )


def inner_products(left_cols, right_cols):
    return lax.dot_general(
        left_cols, right_cols, (((0,), (0,)), ((), ())), preferred_element_type=jnp.float32
    )


def tile_pairs():
    pairs = []
    for row_tile in range(4):
        for col_tile in range(row_tile, 4):
            pairs.append((row_tile, col_tile))
    return pairs


def tile_grams(left_cols, right_cols, tile_width):
    tile_list = []
    for row_tile, col_tile in tile_pairs():
        first = left_cols[:, row_tile * tile_width : (row_tile + 1) * tile_width]
        second = right_cols[:, col_tile * tile_width : (col_tile + 1) * tile_width]
        tile_list.append(inner_products(first, second))
    return jnp.stack(tile_list)


def rebuild(tile_stack):
    pairs = tile_pairs()
    band_rows = []
    for row_tile in range(4):
        band_row = []
        for col_tile in range(4):
            if row_tile <= col_tile:
                band_row.append(tile_stack[pairs.index((row_tile, col_tile))])
            else:
                band_row.append(jnp.transpose(tile_stack[pairs.index((col_tile, row_tile))]))
        band_rows.append(jnp.concatenate(band_row, axis=1))
    return jnp.concatenate(band_rows, axis=0)


def shared_solve(rest_grams, rest_crosses, shrinkage, counts):
    member_count = rest_grams.shape[1]
    width = rest_grams.shape[-1]
    traits = rest_crosses.shape[-1]
    ridge_count = shrinkage.shape[0]
    systems = FOLDS * member_count * ridge_count
    devices = lax.axis_size("sample")
    share = -(-systems // devices)
    flat_grams = rest_grams.reshape(FOLDS * member_count, width, width)
    flat_crosses = rest_crosses.reshape(FOLDS * member_count, width, traits)
    flat_counts = jnp.repeat(counts, member_count)
    owned_ids = lax.axis_index("sample") * share + lax.broadcasted_iota(jnp.int32, (share,), 0)
    owned_ids = jnp.minimum(owned_ids, systems - 1)
    pair_ids = owned_ids // ridge_count
    ridge_ids = owned_ids % ridge_count
    chosen_counts = jnp.take(flat_counts, pair_ids, axis=0)
    system = jnp.take(flat_grams, pair_ids, axis=0) / chosen_counts[:, None, None]
    target = jnp.take(flat_crosses, pair_ids, axis=0) / chosen_counts[:, None, None]
    identity = jnp.eye(width, dtype=jnp.float32)
    full = system + jnp.take(shrinkage, ridge_ids, axis=0)[:, None, None] * identity
    factor = jnp.linalg.cholesky(full)
    solved = jax.vmap(solve_pair, (0, 0))(factor, target).astype(jnp.bfloat16)
    collected = lax.all_gather(solved, "sample", axis=0, tiled=True)
    return collected[:systems].reshape(FOLDS, member_count, ridge_count, width, traits)


def shards(genotype, allele_freq, phenotype, shrinkage, owner_order):
    sample_rows = genotype.shape[0]
    total_rows = sample_rows * lax.axis_size("sample")
    scaled = standardize(genotype, allele_freq)
    ordered = jnp.take(phenotype, owner_order, axis=1)
    local_blocks = allele_freq.shape[0] // SNPS
    tile_width = SNPS // 4
    column_sets = [scaled[:, member * SNPS : (member + 1) * SNPS] for member in range(local_blocks)]
    bounds = [-(-(k * total_rows) // FOLDS) for k in range(FOLDS + 1)]
    counts = jnp.array(
        [float(total_rows - (bounds[k + 1] - bounds[k])) for k in range(FOLDS)], dtype=jnp.float32
    )
    start_row = lax.axis_index("sample") * sample_rows
    row_ids = start_row + lax.broadcasted_iota(jnp.int32, (sample_rows,), 0)
    fold_of = row_ids * FOLDS // total_rows
    first_fold = start_row * FOLDS // total_rows
    slot_folds = [first_fold, first_fold + 1]
    slot_masks = [fold_of == slot_folds[0], fold_of == slot_folds[1]]
    picked = jnp.minimum(jnp.stack(slot_folds), FOLDS - 1)
    fold_ids = jnp.arange(FOLDS, dtype=jnp.int32)

    def fold_partials(member):
        columns = column_sets[member]
        gram_total = jnp.zeros((FOLDS, 10, tile_width, tile_width), jnp.float32)
        cross_total = jnp.zeros((FOLDS, SNPS, ordered.shape[1]), jnp.float32)
        for slot in range(2):
            masked = jnp.where(slot_masks[slot][:, None], columns, jnp.zeros_like(columns))
            selector = (fold_ids == slot_folds[slot]).astype(jnp.float32)
            gram_total = (
                gram_total
                + selector[:, None, None, None] * tile_grams(masked, columns, tile_width)[None]
            )
            cross_total = (
                cross_total + selector[:, None, None] * inner_products(masked, ordered)[None]
            )
        return (gram_total, cross_total)

    def weights_for(members):
        parts = [fold_partials(member) for member in members]
        grams = jnp.stack([item[0] for item in parts], axis=1)
        crosses = jnp.stack([item[1] for item in parts], axis=1)
        summed_grams, summed_crosses = lax.psum((grams, crosses), "sample")
        whole = jax.vmap(jax.vmap(rebuild))(summed_grams)
        rest_grams = jnp.sum(whole, axis=0)[None] - whole
        rest_crosses = jnp.sum(summed_crosses, axis=0)[None] - summed_crosses
        every_weights = shared_solve(rest_grams, rest_crosses, shrinkage, counts)
        return jnp.take(every_weights, picked, axis=0)

    def fold_predictions(member, slot_weights):
        columns = column_sets[member]
        lower = predict(columns, slot_weights[0])
        upper = predict(columns, slot_weights[1])
        return jnp.where(slot_masks[1][None, None, :], upper, lower)

    weights = weights_for(list(range(local_blocks)))
    local_preds = jnp.concatenate(
        [fold_predictions(member, weights[:, member]) for member in range(local_blocks)], axis=1
    )
    return lax.all_to_all(local_preds, "block", split_axis=0, concat_axis=1, tiled=True)


def solution(mesh):
    in_specs = (P("sample", "block"), P("block"), P("sample", None), P(), P())
    out_specs = P("block", None, "sample")
    return jax.shard_map(shards, mesh=mesh, in_specs=in_specs, out_specs=out_specs, check_vma=False)
```

profile of v0, /device:TPU:0, one launch (start us, length us, event | category | flops | bytes accessed | tf_op | source)
XLA Modules:
  0.0 596.3 jit_solution(1321422785324491491)
XLA Ops:
  8.6 2.7 divide_convert_fusion
  31.1 3.5 pad_maximum_fusion
  40.3 146.0 %all-reduce.6.cloned.1.call-done = (f32[5,2,10,125,125]{4,3,1,0,2:T(8,128)}, f32[5,2,500,16]{2,3,1,0:T(8,128)}) async-done(((f32[5,2,10,125,125]{4,3,1,0,2:T(8,128)}, f32[5,2,500,16]{2,3,1,0:T(8,128)}), (f32[5,2,10,125,125]{4,3,1,0,2:T(8,128)}, f32[5,2,500,16]{2,3,1,0:T(8,128)})) %all-reduce.6.cloned.1.call-update) | async-done | bytes 6570016 | tf_op jit(solution)/shard_map/psum | solution.py:133
  186.3 7.2 %slice_bitcast_fusion.19 = (f32[5,2,125,125]{3,2,1,0:T(8,128)}, f32[5,2,125,125]{3,2,1,0:T(8,128)}, f32[5,2,125,125]{2,3,1,0:T(8,128)}, f32[5,2,125,125]{3,2,1,0...) fusion(f32[5,2,10,125,125]{4,3,1,0,2:T(8,128)} %get-tuple-eleme, ...), kind=kLoop, calls=%fused_computation.355 | loop fusion | bytes 18125000 | tf_op jit(solution)/shard_map/vmap(vmap())/squeeze | solution.py:59
  207.5 3.1 pad_maximum_fusion.1
  210.6 3.3 copy.246
  214.0 12.1 %maximum_reduce_fusion = f32[2,500,500]{2,1,0:T(8,128)S(1)} fusion(f32[5,2,125,125]{3,2,1,0:T(8,128)} %get-tuple-element.37, f32[5,2,125,125]{3,2,1,0:T(8,128)} %copy.245, f32[5,2,125,125]{3,2,1,0:T(8,128)S(1)} %bitcast.329, f32[5,2,125,125]{3,2,1,0:T(8,128)} %copy.244, f32[5,2,125,125]{3,2,1,0:T(8,128)} %get-tuple-element.33, ...), kind=kLoop, calls=%fused_computation.8 | loop fusion | flops 32000000 | bytes 12000000 | tf_op jit(solution)/shard_map/reduce_sum | solution.py:135
  226.2 43.5 %maximum_subtract_fusion = f32[10,500,500]{2,1,0:T(8,128)} fusion(f32[10,125,125]{2,1,0:T(8,128)S(1)} %bitcast.345, f32[10,125,125]{2,1,0:T(8,128)S(1)} %bitcast.338, f32[10,125,125]{2,1,0:T(8,128)S(1)} %bitcast.330, f32[10,125,125]{2,1,0:T(8,128)S(1)} %bitcast.339, f32[10,125,125]{2,1,0:T(8,128)S(1)} %bitcast.344, f32[10,125,125]{2,1,0:T(8,128)S(1)} %bitcast.343, ...), kind=kLoop, calls=%fused_computation.9 | loop fusion | flops 40000000 | bytes 22000000 | tf_op jit(solution)/shard_map/sub | solution.py:135
  269.8 5.9 gather_fusion
  275.7 3.2 select_divide_fusion
  278.9 3.0 copy.256
  281.9 3.4 fusion.1
  286.7 23.7 %custom-call.38 = f32[2,128,128]{2,1,0:T(8,128)S(1)} custom-call(f32[2,128,128]{2,1,0:T(8,128)S(1)} %copy.257), custom_call_target="Cholesky" | custom-call | tf_op jit(solution)/shard_map/jit(cholesky)/cholesky | solution.py:86
  311.9 19.7 %custom-call.39 = f32[2,1,128,128]{2,3,1,0:T(8,128)S(1)} custom-call(f32[2,1,128,128]{3,2,1,0:T(8,128)S(1)} %select_bitcast_fusion.2), custom_call_target="InvertDiagBlocksLowerTriangular" | custom-call | tf_op jit(solution)/shard_map/jit(cholesky)/cholesky | solution.py:86
  331.6 2.6 constant_dynamic-update-slice_fusion.3
  335.9 23.5 %custom-call.40 = f32[2,128,128]{2,1,0:T(8,128)S(1)} custom-call(f32[2,128,128]{2,1,0:T(8,128)S(1)} %copy.262), custom_call_target="Cholesky" | custom-call | tf_op jit(solution)/shard_map/jit(cholesky)/cholesky | solution.py:86
  360.1 20.1 %custom-call.41 = f32[2,1,128,128]{2,3,1,0:T(8,128)S(1)} custom-call(f32[2,1,128,128]{3,2,1,0:T(8,128)S(1)} %get-tuple-element.59), custom_call_target="InvertDiagBlocksLowerTriangular" | custom-call | tf_op jit(solution)/shard_map/jit(cholesky)/cholesky | solution.py:86
  383.5 23.5 %custom-call.42 = f32[2,128,128]{2,1,0:T(8,128)S(1)} custom-call(f32[2,128,128]{2,1,0:T(8,128)S(1)} %copy.267), custom_call_target="Cholesky" | custom-call | tf_op jit(solution)/shard_map/jit(cholesky)/cholesky | solution.py:86
  407.7 19.7 %custom-call.43 = f32[2,1,128,128]{2,3,1,0:T(8,128)S(1)} custom-call(f32[2,1,128,128]{3,2,1,0:T(8,128)S(1)} %get-tuple-element.57), custom_call_target="InvertDiagBlocksLowerTriangular" | custom-call | tf_op jit(solution)/shard_map/jit(cholesky)/cholesky | solution.py:86
  430.2 21.5 %custom-call.44 = f32[2,116,116]{2,1,0:T(8,128)S(1)} custom-call(f32[2,116,116]{2,1,0:T(8,128)S(1)} %copy.271), custom_call_target="Cholesky" | custom-call | tf_op jit(solution)/shard_map/jit(cholesky)/cholesky | solution.py:86
  456.2 9.2 %while.1 = (s32[]{:T(128)}, f32[2,500,500]{2,1,0:T(8,128)}, s32[3,2]{0,1:T(2,128)S(1)}, f32[3,2,128,128]{3,2,0,1:T(8,128)S(1)}, s32[]{:T(128)}) while((s32[]{:T(128)}, f32[2,500,500]{2,1,0:T(8,128)}, s32[3,2]{0,1:T(2,128)S(1)}, f32[3,2,128,128]{3,2,0,1:T(8,128)S(1)}, s32[]{:T(128)}) %tuple.71), condition=%wide.while_cond, body=%wide.while_body.sunk | while | flops 2 | bytes 262261 | solution.py:16
  466.5 79.4 %custom-call.45 = f32[2,4,128,128]{2,3,1,0:T(8,128)S(1)} custom-call(f32[2,4,128,128]{3,2,1,0:T(8,128)} %pad_maximum_fusion.2), custom_call_target="InvertDiagBlocksLowerTriangular" | custom-call | tf_op jit(solution)/shard_map/vmap(jit(_cho_solve))/triangular_solve | solution.py:16
  556.7 21.9 %all_gather.3 = bf16[32,500,16]{1,2,0:T(8,128)(2,1)S(1)} all-gather(bf16[2,500,16]{1,2,0:T(8,128)(2,1)S(1)} %pad_maximum_fusion.5), channel_id=1, replica_groups=mesh['sample'=16,'block'=2] {'sample'}, dimensions={0}, use_global_device_ids=true | all-gather | bytes 544000 | tf_op jit(solution)/shard_map/all_gather | solution.py:88
  581.5 7.0 %all_to_all.18 = bf16[16,4,1024]{2,1,0:T(4,128)(2,1)S(1)} all-to-all(bf16[16,4,1024]{2,1,0:T(4,128)(2,1)S(1)} %pad_maximum_fusion.4), channel_id=1, replica_groups=mesh['sample'=16,'block'=2] {'block'}, dimensions={0} | all-to-all | bytes 262144 | tf_op jit(solution)/shard_map/all_to_all | solution.py:150
  (229 shorter events, 82.4 us)
Async XLA Ops:
  6.5 8.1 %copy-start = (bf16[1024,16]{0,1:T(8,128)(2,1)S(1)}, bf16[1024,16]{0,1:T(8,128)(2,1)}, u32[]{:S(2)}) copy-start(bf16[1024,16]{0,1:T(8,128)(2,1)} %param.8) | copy-start | bytes 98308
  6.5 179.8 %all-reduce.6.cloned.1.call-start = ((), (), s32[]{:S(2)}) async-start(), calls=%async_computation.1 | async-start | bytes 13762560 | tf_op jit(solution)/shard_map/psum | solution.py:133
  12.6 2.0 copy-start.17
  15.2 3.3 copy-start.14
  193.5 5.9 copy-start.7
  213.9 12.2 %copy-start.4 = (f32[5,2,1,125,125]{4,3,1,0,2:T(8,128)S(1)}, f32[5,2,1,125,125]{4,3,1,0,2:T(8,128)}, u32[]{:S(2)}) copy-start(f32[5,2,1,125,125]{4,3,1,0,2:T(8,128)} %get-tuple-element.38) | copy-start | bytes 1875004
  213.9 12.3 %copy-start.5 = (f32[5,2,1,125,125]{4,3,1,0,2:T(8,128)S(1)}, f32[5,2,1,125,125]{4,3,1,0,2:T(8,128)}, u32[]{:S(2)}) copy-start(f32[5,2,1,125,125]{4,3,1,0,2:T(8,128)} %get-tuple-element.39) | copy-start | bytes 1875004
  213.9 12.3 %copy-start.6 = (f32[5,2,1,125,125]{4,3,1,0,2:T(8,128)S(1)}, f32[5,2,1,125,125]{4,3,1,0,2:T(8,128)}, u32[]{:S(2)}) copy-start(f32[5,2,1,125,125]{4,3,1,0,2:T(8,128)} %get-tuple-element.40) | copy-start | bytes 1875004
  213.9 12.3 %copy-start.8 = (f32[5,2,1,125,125]{4,3,1,0,2:T(8,128)S(1)}, f32[5,2,1,125,125]{4,3,1,0,2:T(8,128)}, u32[]{:S(2)}) copy-start(f32[5,2,1,125,125]{4,3,1,0,2:T(8,128)} %copy-done.7) | copy-start | bytes 1875004
  213.9 12.3 %copy-start.9 = (f32[5,2,125,125]{3,2,1,0:T(8,128)S(1)}, f32[5,2,125,125]{3,2,1,0:T(8,128)}, u32[]{:S(2)}) copy-start(f32[5,2,125,125]{3,2,1,0:T(8,128)} %copy.245) | copy-start | bytes 1875004
  213.9 12.3 %copy-start.10 = (f32[5,2,125,125]{3,2,1,0:T(8,128)S(1)}, f32[5,2,125,125]{3,2,1,0:T(8,128)}, u32[]{:S(2)}) copy-start(f32[5,2,125,125]{3,2,1,0:T(8,128)} %copy.244) | copy-start | bytes 1875004
  213.9 12.3 %copy-start.11 = (f32[5,2,1,125,125]{3,4,1,0,2:T(8,128)S(1)}, f32[5,2,1,125,125]{3,4,1,0,2:T(8,128)}, u32[]{:S(2)}) copy-start(f32[5,2,1,125,125]{3,4,1,0,2:T(8,128)} %copy.306) | copy-start | bytes 1875004
  213.9 12.3 %copy-start.19 = (f32[5,2,1,125,125]{4,3,1,0,2:T(8,128)S(1)}, f32[5,2,1,125,125]{4,3,1,0,2:T(8,128)}, u32[]{:S(2)}) copy-start(f32[5,2,1,125,125]{4,3,1,0,2:T(8,128)} %get-tuple-element.41) | copy-start | bytes 1875004
  213.9 12.3 %copy-start.20 = (f32[5,2,1,125,125]{4,3,1,0,2:T(8,128)S(1)}, f32[5,2,1,125,125]{4,3,1,0,2:T(8,128)}, u32[]{:S(2)}) copy-start(f32[5,2,1,125,125]{4,3,1,0,2:T(8,128)} %get-tuple-element.42) | copy-start | bytes 1875004
  213.9 12.3 %copy-start.21 = (f32[5,2,1,125,125]{4,3,1,0,2:T(8,128)S(1)}, f32[5,2,1,125,125]{4,3,1,0,2:T(8,128)}, u32[]{:S(2)}) copy-start(f32[5,2,1,125,125]{4,3,1,0,2:T(8,128)} %get-tuple-element.43) | copy-start | bytes 1875004
  213.9 12.3 %copy-start.22 = (f32[5,2,1,125,125]{4,3,1,0,2:T(8,128)S(1)}, f32[5,2,1,125,125]{4,3,1,0,2:T(8,128)}, u32[]{:S(2)}) copy-start(f32[5,2,1,125,125]{4,3,1,0,2:T(8,128)} %get-tuple-element.44) | copy-start | bytes 1875004
  213.9 12.3 %copy-start.23 = (f32[5,2,1,125,125]{4,3,1,0,2:T(8,128)S(1)}, f32[5,2,1,125,125]{4,3,1,0,2:T(8,128)}, u32[]{:S(2)}) copy-start(f32[5,2,1,125,125]{4,3,1,0,2:T(8,128)} %get-tuple-element.46) | copy-start | bytes 1875004
  214.0 12.3 %copy-start.24 = (f32[5,2,1,125,125]{4,3,1,0,2:T(8,128)S(1)}, f32[5,2,1,125,125]{4,3,1,0,2:T(8,128)}, u32[]{:S(2)}) copy-start(f32[5,2,1,125,125]{4,3,1,0,2:T(8,128)} %slice.448) | copy-start | bytes 1875004
  214.0 12.3 %copy-start.25 = (f32[5,2,125,125]{3,2,1,0:T(8,128)S(1)}, f32[5,2,125,125]{3,2,1,0:T(8,128)}, u32[]{:S(2)}) copy-start(f32[5,2,125,125]{3,2,1,0:T(8,128)} %copy.250) | copy-start | bytes 1875004
  278.9 3.0 copy-start.13
  381.5 71.4 %copy-start.27 = (pred[500,500]{1,0:T(8,128)(4,1)S(1)}, pred[500,500]{1,0:T(8,128)(4,1)}, u32[]{:S(2)}) copy-start(pred[500,500]{1,0:T(8,128)(4,1)} %iota_compare_fusion.2) | copy-start | bytes 750004
  452.9 3.3 copy-start.30
  454.9 91.0 %copy-start.26 = (f32[5,2,500,16]{2,3,1,0:T(8,128)S(1)}, f32[5,2,500,16]{2,3,1,0:T(8,128)}, u32[]{:S(2)}) copy-start(f32[5,2,500,16]{2,3,1,0:T(8,128)} %get-tuple-element.25) | copy-start | bytes 960004
  580.7 8.5 %copy-start.1 = (bf16[1024,16]{0,1:T(8,128)(2,1)S(1)}, bf16[1024,16]{0,1:T(8,128)(2,1)}, u32[]{:S(2)}) copy-start(bf16[1024,16]{0,1:T(8,128)(2,1)} %param.8) | copy-start | bytes 98308
  (9 other events, 11.5 us)
Sparse Core Ops, SparseCore 0:
  35.7 150.5 all-reduce.5
where the time goes:
time: 606 us; the launch traced here: 596 us
  other arithmetic  316 us (52%)
  waiting for transfers between devices  146 us (24%)
  local copies, waits for them, and re-layouts  53.2 us (9%)
  matrix products  37.1 us (6%)
  blocking collectives  28.9 us (5%)
  between operations  14.6 us (2%)
    another operation x18, other arithmetic, shared_solve(): factor = jnp.linalg.cholesky(full)  154 us
    psum x1, waiting for transfers between devices, weights_for(): summed_grams, summed_crosses = lax.psum((grams, crosses), 'sample')  146 us
    another operation x9, other arithmetic, solve_pair(): return jax.scipy.linalg.cho_solve((factor, True), target)  83.2 us
    sub x1, other arithmetic, weights_for(): rest_grams = jnp.sum(whole, axis=0)[None] - whole  43.5 us
    all_gather x1, blocking collectives, shared_solve(): collected = lax.all_gather(solved, 'sample', axis=0, tiled=True)  21.9 us
    dot_general x44, matrix products, inner_products(): lax.dot_general(left_cols, right_cols, (((0,), (0,)), ((), ())), preferre...  15.5 us
    reduce_sum x1, other arithmetic, weights_for(): rest_grams = jnp.sum(whole, axis=0)[None] - whole  12.1 us
  transfers between devices with their start and end apart: 1, of which 1 were waited for; matrix products, arithmetic and copies ran while one was open for 1% of the time, Pallas kernels for 0%

commit v1 on v0

--- a/solution.py
+++ b/solution.py
@@ -85,7 +85,14 @@
     full = system + jnp.take(shrinkage, ridge_ids, axis=0)[:, None, None] * identity
     factor = jnp.linalg.cholesky(full)
     solved = jax.vmap(solve_pair, (0, 0))(factor, target).astype(jnp.bfloat16)
-    collected = lax.all_gather(solved, "sample", axis=0, tiled=True)
+    ways = lax.axis_size("sample")
+    pieces = [solved]
+    for far in range(1, ways):
+        pieces.append(
+            lax.ppermute(pieces[far - 1], "sample", [(d, (d - 1) % ways) for d in range(ways)])
+        )
+    line = jnp.concatenate(pieces, axis=0)
+    collected = jnp.roll(line, lax.axis_index("sample") * solved.shape[0], axis=0)
     return collected[:systems].reshape(FOLDS, member_count, ridge_count, width, traits)
 
 

time: 606 us -> 685 us (1.13)
  starting transfers between devices: 0.01 us -> 64.9 us
  blocking collectives: 28.9 us -> 7.01 us
  local copies, waits for them, and re-layouts: 53.2 us -> 72.3 us
  waiting for transfers between devices: 146 us -> 162 us
    ppermute x0 -> x15, starting transfers between devices: none -> 64.9 us  [shared_solve(): lax.ppermute(pieces[far - 1], 'sample', [(d, (d - 1) % ways) for d in ran...]
    all_gather x1 -> x0, blocking collectives: 21.9 us -> none  [shared_solve(): collected = lax.all_gather(solved, 'sample', axis=0, tiled=True)]
    unnamed x68 -> x97, local copies, waits for them, and re-layouts: 10.5 us -> 28.1 us
    ppermute x0 -> x15, waiting for transfers between devices: none -> 15.5 us  [shared_solve(): lax.ppermute(pieces[far - 1], 'sample', [(d, (d - 1) % ways) for d in ran...]
  transfers between devices with their start and end apart: 1 -> 16, of which waited for: 1 -> 16; matrix products, arithmetic and copies ran while one was open for 1% -> 2% of each run, Pallas kernels for 0% -> 0%
where the time goes in v1:
time: 685 us; the launch traced here: 675 us
  other arithmetic  317 us (46%)
  waiting for transfers between devices  162 us (24%)
  local copies, waits for them, and re-layouts  72.3 us (11%)
  starting transfers between devices  64.9 us (9%)
  matrix products  37.3 us (5%)
  between operations  14.6 us (2%)
  blocking collectives  7.01 us (1%)
    another operation x18, other arithmetic, shared_solve(): factor = jnp.linalg.cholesky(full)  154 us
    psum x1, waiting for transfers between devices, weights_for(): summed_grams, summed_crosses = lax.psum((grams, crosses), 'sample')  146 us
    another operation x9, other arithmetic, solve_pair(): return jax.scipy.linalg.cho_solve((factor, True), target)  83.8 us
    ppermute x15, starting transfers between devices, shared_solve(): lax.ppermute(pieces[far - 1], 'sample', [(d, (d - 1) % ways) for d in ran...  64.9 us
    sub x1, other arithmetic, weights_for(): rest_grams = jnp.sum(whole, axis=0)[None] - whole  43.5 us
    unnamed x97, local copies, waits for them, and re-layouts  28.1 us
    dot_general x44, matrix products, inner_products(): lax.dot_general(left_cols, right_cols, (((0,), (0,)), ((), ())), preferre...  15.6 us
    ppermute x15, waiting for transfers between devices, shared_solve(): lax.ppermute(pieces[far - 1], 'sample', [(d, (d - 1) % ways) for d in ran...  15.5 us
  transfers between devices with their start and end apart: 16, of which 16 were waited for; matrix products, arithmetic and copies ran while one was open for 2% of the time, Pallas kernels for 0%

profile of v1, /device:TPU:0, one launch (start us, length us, event | category | flops | bytes accessed | tf_op | source)
XLA Modules:
  0.0 675.2 jit_solution(2702401880353005571)
XLA Ops:
  40.3 146.1 %all-reduce.6.cloned.1.call-done = (f32[5,2,10,125,125]{4,3,1,0,2:T(8,128)}, f32[5,2,500,16]{2,3,1,0:T(8,128)}) async-done(((f32[5,2,10,125,125]{4,3,1,0,2:T(8,128)}, f32[5,2,500,16]{2,3,1,0:T(8,128)}), (f32[5,2,10,125,125]{4,3,1,0,2:T(8,128)}, f32[5,2,500,16]{2,3,1,0:T(8,128)})) %all-reduce.6.cloned.1.call-update) | async-done | bytes 6570016 | tf_op jit(solution)/shard_map/psum | solution.py:140
  186.4 7.2 %slice_bitcast_fusion.19 = (f32[5,2,125,125]{3,2,1,0:T(8,128)}, f32[5,2,125,125]{3,2,1,0:T(8,128)}, f32[5,2,125,125]{2,3,1,0:T(8,128)}, f32[5,2,125,125]{3,2,1,0...) fusion(f32[5,2,10,125,125]{4,3,1,0,2:T(8,128)} %get-tuple-eleme, ...), kind=kLoop, calls=%fused_computation.388 | loop fusion | bytes 18125000 | tf_op jit(solution)/shard_map/vmap(vmap())/squeeze | solution.py:59
  214.0 12.1 %maximum_reduce_fusion = f32[2,500,500]{2,1,0:T(8,128)S(1)} fusion(f32[5,2,125,125]{3,2,1,0:T(8,128)} %get-tuple-element.37, f32[5,2,125,125]{3,2,1,0:T(8,128)} %copy.195, f32[5,2,125,125]{3,2,1,0:T(8,128)S(1)} %bitcast.329, f32[5,2,125,125]{3,2,1,0:T(8,128)} %copy.194, f32[5,2,125,125]{3,2,1,0:T(8,128)} %get-tuple-element.33, ...), kind=kLoop, calls=%fused_computation.8 | loop fusion | flops 32000000 | bytes 12000000 | tf_op jit(solution)/shard_map/reduce_sum | solution.py:142
  226.3 43.5 %maximum_subtract_fusion = f32[10,500,500]{2,1,0:T(8,128)} fusion(f32[10,125,125]{2,1,0:T(8,128)S(1)} %bitcast.345, f32[10,125,125]{2,1,0:T(8,128)S(1)} %bitcast.338, f32[10,125,125]{2,1,0:T(8,128)S(1)} %bitcast.330, f32[10,125,125]{2,1,0:T(8,128)S(1)} %bitcast.339, f32[10,125,125]{2,1,0:T(8,128)S(1)} %bitcast.344, f32[10,125,125]{2,1,0:T(8,128)S(1)} %bitcast.343, ...), kind=kLoop, calls=%fused_computation.9 | loop fusion | flops 40000000 | bytes 22000000 | tf_op jit(solution)/shard_map/sub | solution.py:142
  269.8 6.0 gather_fusion
  286.8 23.7 %custom-call.38 = f32[2,128,128]{2,1,0:T(8,128)S(1)} custom-call(f32[2,128,128]{2,1,0:T(8,128)S(1)} %copy.207), custom_call_target="Cholesky" | custom-call | tf_op jit(solution)/shard_map/jit(cholesky)/cholesky | solution.py:86
  312.0 19.7 %custom-call.39 = f32[2,1,128,128]{2,3,1,0:T(8,128)S(1)} custom-call(f32[2,1,128,128]{3,2,1,0:T(8,128)S(1)} %select_bitcast_fusion.2), custom_call_target="InvertDiagBlocksLowerTriangular" | custom-call | tf_op jit(solution)/shard_map/jit(cholesky)/cholesky | solution.py:86
  336.1 23.5 %custom-call.40 = f32[2,128,128]{2,1,0:T(8,128)S(1)} custom-call(f32[2,128,128]{2,1,0:T(8,128)S(1)} %copy.212), custom_call_target="Cholesky" | custom-call | tf_op jit(solution)/shard_map/jit(cholesky)/cholesky | solution.py:86
  360.2 20.1 %custom-call.41 = f32[2,1,128,128]{2,3,1,0:T(8,128)S(1)} custom-call(f32[2,1,128,128]{3,2,1,0:T(8,128)S(1)} %get-tuple-element.59), custom_call_target="InvertDiagBlocksLowerTriangular" | custom-call | tf_op jit(solution)/shard_map/jit(cholesky)/cholesky | solution.py:86
  383.7 23.5 %custom-call.42 = f32[2,128,128]{2,1,0:T(8,128)S(1)} custom-call(f32[2,128,128]{2,1,0:T(8,128)S(1)} %copy.217), custom_call_target="Cholesky" | custom-call | tf_op jit(solution)/shard_map/jit(cholesky)/cholesky | solution.py:86
  407.9 19.7 %custom-call.43 = f32[2,1,128,128]{2,3,1,0:T(8,128)S(1)} custom-call(f32[2,1,128,128]{3,2,1,0:T(8,128)S(1)} %get-tuple-element.57), custom_call_target="InvertDiagBlocksLowerTriangular" | custom-call | tf_op jit(solution)/shard_map/jit(cholesky)/cholesky | solution.py:86
  430.5 21.5 %custom-call.44 = f32[2,116,116]{2,1,0:T(8,128)S(1)} custom-call(f32[2,116,116]{2,1,0:T(8,128)S(1)} %copy.221), custom_call_target="Cholesky" | custom-call | tf_op jit(solution)/shard_map/jit(cholesky)/cholesky | solution.py:86
  456.5 9.1 %while.1 = (s32[]{:T(128)}, f32[2,500,500]{2,1,0:T(8,128)}, s32[3,2]{0,1:T(2,128)S(1)}, f32[3,2,128,128]{3,2,0,1:T(8,128)S(1)}, s32[]{:T(128)}) while((s32[]{:T(128)}, f32[2,500,500]{2,1,0:T(8,128)}, s32[3,2]{0,1:T(2,128)S(1)}, f32[3,2,128,128]{3,2,0,1:T(8,128)S(1)}, s32[]{:T(128)}) %tuple.73), condition=%wide.while_cond, body=%wide.while_body.sunk | while | flops 2 | bytes 262261 | solution.py:16
  466.6 79.4 %custom-call.45 = f32[2,4,128,128]{2,3,1,0:T(8,128)S(1)} custom-call(f32[2,4,128,128]{3,2,1,0:T(8,128)} %pad_maximum_fusion.2), custom_call_target="InvertDiagBlocksLowerTriangular" | custom-call | tf_op jit(solution)/shard_map/vmap(jit(_cho_solve))/triangular_solve | solution.py:16
  561.7 4.4 collective-permute-start.1
  567.7 4.4 collective-permute-start.2
  573.8 4.4 collective-permute-start.3
  579.8 4.4 collective-permute-start.4
  585.9 4.4 collective-permute-start.5
  591.9 4.4 collective-permute-start.6
  597.9 4.4 collective-permute-start.7
  604.0 4.4 collective-permute-start.8
  622.1 4.4 collective-permute-start.11
  660.4 7.0 %all_to_all.18 = bf16[16,4,1024]{2,1,0:T(4,128)(2,1)S(1)} all-to-all(bf16[16,4,1024]{2,1,0:T(4,128)(2,1)S(1)} %pad_maximum_fusion.4), channel_id=1, replica_groups=mesh['sample'=16,'block'=2] {'block'}, dimensions={0} | all-to-all | bytes 262144 | tf_op jit(solution)/shard_map/all_to_all | solution.py:157
  (288 shorter events, 167.8 us)
Async XLA Ops:
  6.5 179.8 %all-reduce.6.cloned.1.call-start = ((), (), s32[]{:S(2)}) async-start(), calls=%async_computation.1 | async-start | bytes 13762560 | tf_op jit(solution)/shard_map/psum | solution.py:140
  213.9 12.3 %copy-start.9 = (f32[5,2,125,125]{3,2,1,0:T(8,128)S(1)}, f32[5,2,125,125]{3,2,1,0:T(8,128)}, u32[]{:S(2)}) copy-start(f32[5,2,125,125]{3,2,1,0:T(8,128)} %copy.195) | copy-start | bytes 1875004
  213.9 12.3 %copy-start.10 = (f32[5,2,125,125]{3,2,1,0:T(8,128)S(1)}, f32[5,2,125,125]{3,2,1,0:T(8,128)}, u32[]{:S(2)}) copy-start(f32[5,2,125,125]{3,2,1,0:T(8,128)} %copy.194) | copy-start | bytes 1875004
  213.9 12.3 %copy-start.11 = (f32[5,2,1,125,125]{3,4,1,0,2:T(8,128)S(1)}, f32[5,2,1,125,125]{3,4,1,0,2:T(8,128)}, u32[]{:S(2)}) copy-start(f32[5,2,1,125,125]{3,4,1,0,2:T(8,128)} %copy.256) | copy-start | bytes 1875004
  214.0 12.3 %copy-start.19 = (f32[5,2,1,125,125]{4,3,1,0,2:T(8,128)S(1)}, f32[5,2,1,125,125]{4,3,1,0,2:T(8,128)}, u32[]{:S(2)}) copy-start(f32[5,2,1,125,125]{4,3,1,0,2:T(8,128)} %get-tuple-element.41) | copy-start | bytes 1875004
  214.0 12.3 %copy-start.20 = (f32[5,2,1,125,125]{4,3,1,0,2:T(8,128)S(1)}, f32[5,2,1,125,125]{4,3,1,0,2:T(8,128)}, u32[]{:S(2)}) copy-start(f32[5,2,1,125,125]{4,3,1,0,2:T(8,128)} %get-tuple-element.42) | copy-start | bytes 1875004
  214.0 12.3 %copy-start.21 = (f32[5,2,1,125,125]{4,3,1,0,2:T(8,128)S(1)}, f32[5,2,1,125,125]{4,3,1,0,2:T(8,128)}, u32[]{:S(2)}) copy-start(f32[5,2,1,125,125]{4,3,1,0,2:T(8,128)} %get-tuple-element.43) | copy-start | bytes 1875004
  381.6 71.5 %copy-start.27 = (pred[500,500]{1,0:T(8,128)(4,1)S(1)}, pred[500,500]{1,0:T(8,128)(4,1)}, u32[]{:S(2)}) copy-start(pred[500,500]{1,0:T(8,128)(4,1)} %iota_compare_fusion.2) | copy-start | bytes 750004
  455.2 90.8 %copy-start.26 = (f32[5,2,500,16]{2,3,1,0:T(8,128)S(1)}, f32[5,2,500,16]{2,3,1,0:T(8,128)}, u32[]{:S(2)}) copy-start(f32[5,2,500,16]{2,3,1,0:T(8,128)} %get-tuple-element.25) | copy-start | bytes 960004
  557.4 4.3 collective-permute-start
  561.7 6.0 collective-permute-start.1
  567.7 6.0 collective-permute-start.2
  573.8 6.0 collective-permute-start.3
  579.8 6.0 collective-permute-start.4
  585.9 6.0 collective-permute-start.5
  591.9 6.0 collective-permute-start.6
  597.9 6.0 collective-permute-start.7
  604.0 6.0 collective-permute-start.8
  610.0 6.0 collective-permute-start.9
  616.0 6.0 collective-permute-start.10
  622.1 6.0 collective-permute-start.11
  628.1 6.0 collective-permute-start.12
  634.1 6.0 collective-permute-start.13
  640.2 6.0 collective-permute-start.14
  (24 other events, 144.1 us)
Sparse Core Ops, SparseCore 0:
  35.8 150.5 all-reduce.5
